TPU v7x, 128 devices: a whole 4x4x4 slice. The times are simulated.
128 devices in a mesh: section: 8 (over y, core), seq: 16 (over z, x).
Axes of the slice: x: 4, y: 4, z: 4, core: 2. Of those that a mesh axis runs over, the one named last changes fastest.
Arguments:
- hidden: bfloat16 [2, 2048, 4096], P(None, 'seq'), may hold values from -6 to 6
- queries: bfloat16 [8, 2, 2048, 4096], P('section', None, 'seq'), may hold values from -6 to 6
- gain: float32 [8, 4096], P('section'), may hold values from 0.5 to 2
- key_weight: bfloat16 [8, 4096, 512], P('section'), may hold values from -1 to 1
- value_weight: bfloat16 [8, 4096, 512], P('section'), may hold values from -0.09375 to 0.09375
- tree_ids: int32 [2, 2048], replicated, may hold values from 0 to 7, as said below
- branch_ids: int32 [2, 2048], replicated, may hold values from 0 to 2, as said below
- span_order: int32 [2, 32], replicated, may hold values from 0 to 31, each once within a row
Outputs:
- layer_out: bfloat16 [8, 2, 2048, 4096], P('section', None, 'seq')
Inputs may be any that keep to these rules, and one draw needn't show every extreme that they name: `tree_ids`: in each microbatch nondecreasing along the packed positions, every value of 0 to 7 present, each tree a multiple of 16 positions long. `branch_ids`: within each tree the prompt, chosen and rejected positions come in that order, each branch one position or more. `span_order`: each row is a permutation of 0 to 31.
All inputs are finite; a program needn't handle non-finite values.
Results may differ from a plain program's by a relative error of at most 0.02.
Values may be sent and summed in bfloat16 or wider, within the bound.
No kernel may reach another device: no remote copies, remote signals or barrier semaphores. Data moves between devices by JAX's collectives and lax.ppermute only.
A program may use at most 128 MiB of HBM per device.

v0:
```python
import math
import jax
import jax.numpy as jnp
from jax import lax
from jax.sharding import PartitionSpec as P

HQ = 32
HK = 4
HD = 128
SPAN = 64
rope_base = 500000.0


def from_behind(value, axis, by):
    size = lax.axis_size(axis)
    pairs = [(i, i + by) for i in range(size) if 0 <= i + by < size]
    return lax.ppermute(value, axis, pairs)


def frequencies():
    exponent = jnp.arange(HD // 2, dtype=jnp.float32) * (2.0 / HD)
    return jnp.power(jnp.float32(rope_base), -exponent)


def rotate(vectors, angles):
    half_dim = vectors.shape[-1] // 2
    cosine = jnp.cos(angles)[..., None, :]
    sine_part = jnp.sin(angles)[..., None, :]
    lower_half = vectors[..., :half_dim]
    upper_half = vectors[..., half_dim:]
    return jnp.concatenate(
        [
            lower_half * cosine - upper_half * sine_part,
            upper_half * cosine + lower_half * sine_part,
        ],
        axis=-1,
    )


def tree_positions(tree_ids, branch_ids):
    positions = jnp.arange(tree_ids.shape[1], dtype=jnp.int32)[None, :]
    opening = jnp.concatenate(
        [jnp.ones_like(tree_ids[:, :1]), (tree_ids[:, 1:] != tree_ids[:, :-1]).astype(jnp.int32)],
        axis=1,
    )
    starts = lax.cummax(jnp.where(opening > 0, positions, 0), axis=1)
    chosen = (branch_ids == 1).astype(jnp.int32)
    counted = jnp.cumsum(chosen, axis=1, dtype=jnp.int32)
    before = jnp.take_along_axis(counted - chosen, starts, axis=1)
    skipped = jnp.where(branch_ids == 2, counted - before, 0)
    return positions - starts - skipped


def local(hidden, queries, gain, key_weight, value_weight, tree_ids, branch_ids, span_order):
    section_id = lax.axis_index("section")
    shard_id = lax.axis_index("seq")
    section_count = lax.axis_size("section")
    micro_count, row_count, model_width = hidden.shape
    seq_len = tree_ids.shape[1]
    per_pass = 1
    ratio = HQ // HK
    scale = 1.0 / math.sqrt(HD)
    rotary_all = tree_positions(tree_ids, branch_ids)
    stored_ids = jnp.arange(seq_len, dtype=jnp.int32)
    packed_all = jnp.take(span_order, stored_ids // SPAN, axis=1) * SPAN + stored_ids % SPAN
    inverse = frequencies()
    gain_row = gain[0]
    key_mat = key_weight[0]
    value_mat = value_weight[0]

    def run_layer(current, first_mb, active):
        packed = lax.dynamic_slice_in_dim(packed_all, first_mb, per_pass, 0)
        trees = lax.dynamic_slice_in_dim(tree_ids, first_mb, per_pass, 0)
        branches = lax.dynamic_slice_in_dim(branch_ids, first_mb, per_pass, 0)
        rotary = lax.dynamic_slice_in_dim(rotary_all, first_mb, per_pass, 0)
        own_packed = lax.dynamic_slice_in_dim(packed, shard_id * row_count, row_count, 1)
        own_tree = jnp.take_along_axis(trees, own_packed, axis=1)
        own_branch = jnp.take_along_axis(branches, own_packed, axis=1)
        own_angles = (
            jnp.take_along_axis(rotary, own_packed, axis=1).astype(jnp.float32)[..., None] * inverse
        )
        widened = current.astype(jnp.float32)
        norm_scale = lax.rsqrt(jnp.mean(widened * widened, axis=-1, keepdims=True) + 1e-05)
        normed = (widened * norm_scale * gain_row).astype(jnp.bfloat16)
        flat = normed.reshape(per_pass * row_count, model_width)
        key_proj = jnp.dot(flat, key_mat, preferred_element_type=jnp.float32).reshape(
            per_pass, row_count, HK, HD
        )
        key_rows = (
            rotate(key_proj, own_angles).astype(jnp.bfloat16).reshape(per_pass, row_count, HK * HD)
        )
        value_rows = (
            jnp.dot(flat, value_mat, preferred_element_type=jnp.float32)
            .astype(jnp.bfloat16)
            .reshape(per_pass, row_count, HK * HD)
        )
        query_local = lax.dynamic_slice_in_dim(queries[0], first_mb, per_pass, 0)
        turned = rotate(
            query_local.astype(jnp.float32).reshape(per_pass, row_count, HQ, HD), own_angles
        ).astype(jnp.bfloat16)
        grouped = turned.reshape(per_pass, row_count, HK, ratio, HD)
        start_top = jnp.full((per_pass, HK, ratio, row_count), -jnp.inf, jnp.float32)
        start_sum = jnp.zeros((per_pass, HK, ratio, row_count), jnp.float32)
        start_acc = jnp.zeros((per_pass, HK, ratio, row_count, HD), jnp.float32)
        key_piece = lax.all_gather(key_rows, "seq", axis=1, tiled=True)
        value_piece = lax.all_gather(value_rows, "seq", axis=1, tiled=True)
        piece_len = key_piece.shape[1]
        block_len = math.gcd(piece_len, 512)

        def update(inner, operands):
            row_top, denominator, accum = inner
            key_blk, value_blk, allowed = operands
            scores = (
                jnp.einsum(
                    "grkhd,gskd->gkhrs",
                    grouped,
                    key_blk.reshape(per_pass, block_len, HK, HD),
                    preferred_element_type=jnp.float32,
                )
                * scale
            )
            masked = jnp.where(allowed[:, None, None], scores, -jnp.inf)
            new_top = jnp.maximum(row_top, jnp.max(masked, axis=-1))
            safe_top = jnp.where(jnp.isfinite(new_top), new_top, 0.0)
            weights = jnp.exp(masked - safe_top[..., None])
            rescale = jnp.exp(row_top - safe_top)
            denominator = denominator * rescale + jnp.sum(weights, axis=-1)
            accum = accum * rescale[..., None] + jnp.einsum(
                "gkhrs,gskd->gkhrd",
                weights.astype(jnp.bfloat16),
                value_blk.reshape(per_pass, block_len, HK, HD),
                preferred_element_type=jnp.float32,
            )
            return (new_top, denominator, accum)

        def step(block_id, inner):
            begin = block_id * block_len
            key_blk = lax.dynamic_slice_in_dim(key_piece, begin, block_len, 1)
            value_blk = lax.dynamic_slice_in_dim(value_piece, begin, block_len, 1)
            key_packed = lax.dynamic_slice_in_dim(packed, begin, block_len, 1)
            key_tree = jnp.take_along_axis(trees, key_packed, axis=1)
            key_branch = jnp.take_along_axis(branches, key_packed, axis=1)
            allowed = (
                (own_tree[:, :, None] == key_tree[:, None, :])
                & (key_packed[:, None, :] <= own_packed[:, :, None])
                & (
                    (key_branch[:, None, :] == 0)
                    | (key_branch[:, None, :] == own_branch[:, :, None])
                )
            )
            operands = (key_blk, value_blk, allowed)
            return update(inner, operands)

        def sweep(inner):
            return lax.fori_loop(0, piece_len // block_len, step, inner)

        row_top, denominator, accum = lax.cond(
            active, sweep, lambda inner: inner, (start_top, start_sum, start_acc)
        )
        safe_sum = jnp.where(denominator > 0.0, denominator, 1.0)
        attended = (
            (accum / safe_sum[..., None])
            .transpose(0, 3, 1, 2, 4)
            .reshape(per_pass, row_count, HQ * HD)
            .astype(jnp.bfloat16)
        )
        return (widened + attended.astype(jnp.float32)).astype(jnp.bfloat16)

    tick_count = section_count + micro_count // per_pass - 1

    def advance(step_id, state_pair):
        previous, outputs = state_pair
        incoming = from_behind(previous, "section", 1)
        first_mb = (step_id - section_id) * per_pass
        active = (first_mb >= 0) & (first_mb < micro_count)
        start_at = jnp.clip(first_mb, 0, micro_count - per_pass)
        entering = lax.dynamic_slice_in_dim(hidden, start_at, per_pass, 0)
        current = jnp.where(section_id == 0, entering, incoming)
        computed = run_layer(current, start_at, active)
        result = jnp.where(active, computed, jnp.zeros_like(computed))
        stored = lax.dynamic_update_slice_in_dim(outputs, result, start_at, 0)
        outputs = jnp.where(active, stored, outputs)
        return (result, outputs)

    empty_pass = jnp.zeros((per_pass, row_count, model_width), jnp.bfloat16)
    empty_out = jnp.zeros((micro_count, row_count, model_width), jnp.bfloat16)
    final_pass, outputs = lax.fori_loop(0, tick_count, advance, (empty_pass, empty_out))
    return outputs[None]


def solution(mesh):
    placed = (
        P(None, "seq", None),
        P("section", None, "seq", None),
        P("section", None),
        P("section", None, None),
        P("section", None, None),
        P(),
        P(),
        P(),
    )
    return jax.shard_map(
        local,
        mesh=mesh,
        in_specs=placed,
        out_specs=P("section", None, "seq", None),
        check_vma=False,
    )
```

profile of v0, /device:TPU:25, one launch (start us, length us, event | category | flops | bytes accessed | tf_op | source)
XLA Modules:
  0.0 2184.3 jit_solution(5759646535908856767)
XLA Ops:
  6.5 6.4 copy.28
  15.4 34.9 %gather_fusion.6 = s32[4096]{0:T(1024)S(1)} fusion(s32[2,2048]{1,0:T(2,128)S(1)} %bitcast_subtract_fusion, s32[4096]{0:T(1024)S(1)} %bitcast.243), kind=kCustom, calls=%fused_computation.6 | custom fusion | bytes 65536 | tf_op jit(solution)/shard_map/jit(take_along_axis)/gather | solution.py:49
  50.5 5.5 gather_fusion.5
  58.6 2118.9 %while.41 = (s32[]{:T(128)}, bf16[1,128,4096]{2,1,0:T(8,128)(2,1)}, bf16[2,128,4096]{2,1,0:T(8,128)(2,1)}, s32[]{:T(128)}, pred[]{:T(512)}, /*index=5*/bf16[2,12...) while((s32[]{:T(128)}, bf16[1,128,4096]{2,1,0:T(8,128)(2,1)}, ...), condition=%wide.region_12.15_spmd.clone, body=%wide.region_4.14_spmd.clone.sunk | while | flops 2188912640 | bytes 114081576 | solution.py:187
  69.4 3.7 convolution_convert_fusion.2
  80.2 49.8 %all-gather.7.cloned.1.call-done = bf16[1,2048,512]{1,2,0:T(8,128)(2,1)} async-done(((bf16[1,128,512]{1,2,0:T(8,128)(2,1)}), bf16[1,2048,512]{1,2,0:T(8,128)(2,1)}) %all-gather.7.cloned.1.call-update) | async-done | bytes 2097168 | tf_op jit(solution)/shard_map/while/body/eval_jaxpr/all_gather | solution.py:105
  130.0 46.5 %all-gather.9.cloned.1.call-done = bf16[2048,512]{1,0:T(8,128)(2,1)} async-done(((bf16[128,512]{1,0:T(8,128)(2,1)}), bf16[2048,512]{1,0:T(8,128)(2,1)}) %all-gather.9.cloned.1.call-update) | async-done | bytes 2097168 | tf_op jit(solution)/shard_map/while/body/eval_jaxpr/all_gather | solution.py:106
  197.5 3.5 convolution_bitcast_fusion.2
  201.8 3.7 convolution_convert_fusion.2
  212.5 140.5 %all-gather.7.cloned.1.call-done = bf16[1,2048,512]{1,2,0:T(8,128)(2,1)} async-done(((bf16[1,128,512]{1,2,0:T(8,128)(2,1)}), bf16[1,2048,512]{1,2,0:T(8,128)(2,1)}) %all-gather.7.cloned.1.call-update) | async-done | bytes 2097168 | tf_op jit(solution)/shard_map/while/body/eval_jaxpr/all_gather | solution.py:105
  353.0 46.4 %all-gather.9.cloned.1.call-done = bf16[2048,512]{1,0:T(8,128)(2,1)} async-done(((bf16[128,512]{1,0:T(8,128)(2,1)}), bf16[2048,512]{1,0:T(8,128)(2,1)}) %all-gather.9.cloned.1.call-update) | async-done | bytes 2097168 | tf_op jit(solution)/shard_map/while/body/eval_jaxpr/all_gather | solution.py:106
  420.4 3.5 convolution_bitcast_fusion.2
  424.7 3.7 convolution_convert_fusion.2
  435.4 151.1 %all-gather.7.cloned.1.call-done = bf16[1,2048,512]{1,2,0:T(8,128)(2,1)} async-done(((bf16[1,128,512]{1,2,0:T(8,128)(2,1)}), bf16[1,2048,512]{1,2,0:T(8,128)(2,1)}) %all-gather.7.cloned.1.call-update) | async-done | bytes 2097168 | tf_op jit(solution)/shard_map/while/body/eval_jaxpr/all_gather | solution.py:105
  586.6 46.4 %all-gather.9.cloned.1.call-done = bf16[2048,512]{1,0:T(8,128)(2,1)} async-done(((bf16[128,512]{1,0:T(8,128)(2,1)}), bf16[2048,512]{1,0:T(8,128)(2,1)}) %all-gather.9.cloned.1.call-update) | async-done | bytes 2097168 | tf_op jit(solution)/shard_map/while/body/eval_jaxpr/all_gather | solution.py:106
  658.2 3.7 convolution_convert_fusion.2
  669.0 154.0 %all-gather.7.cloned.1.call-done = bf16[1,2048,512]{1,2,0:T(8,128)(2,1)} async-done(((bf16[1,128,512]{1,2,0:T(8,128)(2,1)}), bf16[1,2048,512]{1,2,0:T(8,128)(2,1)}) %all-gather.7.cloned.1.call-update) | async-done | bytes 2097168 | tf_op jit(solution)/shard_map/while/body/eval_jaxpr/all_gather | solution.py:105
  822.9 46.5 %all-gather.9.cloned.1.call-done = bf16[2048,512]{1,0:T(8,128)(2,1)} async-done(((bf16[128,512]{1,0:T(8,128)(2,1)}), bf16[2048,512]{1,0:T(8,128)(2,1)}) %all-gather.9.cloned.1.call-update) | async-done | bytes 2097168 | tf_op jit(solution)/shard_map/while/body/eval_jaxpr/all_gather | solution.py:106
  894.7 3.7 convolution_convert_fusion.2
  905.4 154.0 %all-gather.7.cloned.1.call-done = bf16[1,2048,512]{1,2,0:T(8,128)(2,1)} async-done(((bf16[1,128,512]{1,2,0:T(8,128)(2,1)}), bf16[1,2048,512]{1,2,0:T(8,128)(2,1)}) %all-gather.7.cloned.1.call-update) | async-done | bytes 2097168 | tf_op jit(solution)/shard_map/while/body/eval_jaxpr/all_gather | solution.py:105
  1059.4 46.4 %all-gather.9.cloned.1.call-done = bf16[2048,512]{1,0:T(8,128)(2,1)} async-done(((bf16[128,512]{1,0:T(8,128)(2,1)}), bf16[2048,512]{1,0:T(8,128)(2,1)}) %all-gather.9.cloned.1.call-update) | async-done | bytes 2097168 | tf_op jit(solution)/shard_map/while/body/eval_jaxpr/all_gather | solution.py:106
  1131.1 3.7 convolution_convert_fusion.2
  1141.8 155.5 %all-gather.7.cloned.1.call-done = bf16[1,2048,512]{1,2,0:T(8,128)(2,1)} async-done(((bf16[1,128,512]{1,2,0:T(8,128)(2,1)}), bf16[1,2048,512]{1,2,0:T(8,128)(2,1)}) %all-gather.7.cloned.1.call-update) | async-done | bytes 2097168 | tf_op jit(solution)/shard_map/while/body/eval_jaxpr/all_gather | solution.py:105
  1297.3 46.4 %all-gather.9.cloned.1.call-done = bf16[2048,512]{1,0:T(8,128)(2,1)} async-done(((bf16[128,512]{1,0:T(8,128)(2,1)}), bf16[2048,512]{1,0:T(8,128)(2,1)}) %all-gather.9.cloned.1.call-update) | async-done | bytes 2097168 | tf_op jit(solution)/shard_map/while/body/eval_jaxpr/all_gather | solution.py:106
  1369.0 3.7 convolution_convert_fusion.2
  1379.7 155.5 %all-gather.7.cloned.1.call-done = bf16[1,2048,512]{1,2,0:T(8,128)(2,1)} async-done(((bf16[1,128,512]{1,2,0:T(8,128)(2,1)}), bf16[1,2048,512]{1,2,0:T(8,128)(2,1)}) %all-gather.7.cloned.1.call-update) | async-done | bytes 2097168 | tf_op jit(solution)/shard_map/while/body/eval_jaxpr/all_gather | solution.py:105
  1535.2 46.4 %all-gather.9.cloned.1.call-done = bf16[2048,512]{1,0:T(8,128)(2,1)} async-done(((bf16[128,512]{1,0:T(8,128)(2,1)}), bf16[2048,512]{1,0:T(8,128)(2,1)}) %all-gather.9.cloned.1.call-update) | async-done | bytes 2097168 | tf_op jit(solution)/shard_map/while/body/eval_jaxpr/all_gather | solution.py:106
  1597.8 111.5 %collective-permute-done = bf16[1,128,4096]{2,1,0:T(8,128)(2,1)S(1)} collective-permute-done((bf16[1,128,4096]{2,1,0:T(8,128)(2,1)S(1)}, bf16[1,128,4096]{2,1,0:T(8,128)(2,1)S(1)}, u32[]{:S(2)}, u32[]{:S(2)}) %collective-permute-start) | collective-permute-done | bytes 1048608 | tf_op jit(solution)/shard_map/while/body/eval_jaxpr/ppermute | solution.py:17
  1711.1 3.5 convolution_bitcast_fusion.2
  1715.4 3.7 convolution_convert_fusion.2
  1726.1 46.7 %all-gather.7.cloned.1.call-done = bf16[1,2048,512]{1,2,0:T(8,128)(2,1)} async-done(((bf16[1,128,512]{1,2,0:T(8,128)(2,1)}), bf16[1,2048,512]{1,2,0:T(8,128)(2,1)}) %all-gather.7.cloned.1.call-update) | async-done | bytes 2097168 | tf_op jit(solution)/shard_map/while/body/eval_jaxpr/all_gather | solution.py:105
  1772.8 46.4 %all-gather.9.cloned.1.call-done = bf16[2048,512]{1,0:T(8,128)(2,1)} async-done(((bf16[128,512]{1,0:T(8,128)(2,1)}), bf16[2048,512]{1,0:T(8,128)(2,1)}) %all-gather.9.cloned.1.call-update) | async-done | bytes 2097168 | tf_op jit(solution)/shard_map/while/body/eval_jaxpr/all_gather | solution.py:106
  1819.1 110.7 %conditional.3 = (f32[1,4,8,128]{3,2,1,0:T(8,128)}, f32[1,4,8,128,128]{4,3,2,1,0:T(8,128)}) conditional(s32[]{:T(128)} %convert_element_type.273, () %tuple.129, (s32[2,2048]{1,0:T(2,128)S(1)}, s32[]{:T(128)}, pred[1,128]{1,0:T(4,128)(4,1)S(1)}, s32[1,2048]{1,0:T(1,128)S(1)}, s32[1,128]{1,0:T(1,128)S(1)}, /*index=5*/s32[1,2048]{1,0:T(1,128)S(1)}, ...), branch_computations={%region_6.7_spmd, %region_7.13_spmd.clone} | conditional | flops 1098833152 | bytes 35224720 | solution.py:157
  1819.2 110.7 %while.40 = (s32[]{:T(128)}, f32[1,4,8,128]{3,2,1,0:T(8,128)S(1)}, f32[1,4,8,128]{3,2,1,0:T(8,128)}, f32[1,4,8,128,128]{4,3,2,1,0:T(8,128)}, s32[1,128]{1,0:T(1,...) while((s32[]{:T(128)}, f32[1,4,8,128]{3,2,1,0:T(8,128)S(1)}, ...), condition=%wide.region_11.12_spmd.clone, body=%wide.region_8.11_spmd.clone.sunk | while | flops 1098832896 | bytes 35205864 | solution.py:155
  1827.0 4.6 fusion.86
  1831.6 5.1 fusion.89
  1838.6 7.3 bitcast_add_fusion.5
  1853.6 4.6 fusion.86
  1858.3 5.1 fusion.89
  1866.0 7.9 bitcast_add_fusion.5
  1881.6 4.6 fusion.86
  1886.3 5.1 fusion.89
  1894.0 7.9 bitcast_add_fusion.5
  1909.6 4.6 fusion.86
  1914.3 5.1 fusion.89
  1922.0 7.9 bitcast_add_fusion.5
  1948.7 3.5 convolution_bitcast_fusion.2
  1953.0 3.7 convolution_convert_fusion.2
  1963.7 46.7 %all-gather.7.cloned.1.call-done = bf16[1,2048,512]{1,2,0:T(8,128)(2,1)} async-done(((bf16[1,128,512]{1,2,0:T(8,128)(2,1)}), bf16[1,2048,512]{1,2,0:T(8,128)(2,1)}) %all-gather.7.cloned.1.call-update) | async-done | bytes 2097168 | tf_op jit(solution)/shard_map/while/body/eval_jaxpr/all_gather | solution.py:105
  2010.4 46.4 %all-gather.9.cloned.1.call-done = bf16[2048,512]{1,0:T(8,128)(2,1)} async-done(((bf16[128,512]{1,0:T(8,128)(2,1)}), bf16[2048,512]{1,0:T(8,128)(2,1)}) %all-gather.9.cloned.1.call-update) | async-done | bytes 2097168 | tf_op jit(solution)/shard_map/while/body/eval_jaxpr/all_gather | solution.py:106
  2056.7 110.7 %conditional.3 = (f32[1,4,8,128]{3,2,1,0:T(8,128)}, f32[1,4,8,128,128]{4,3,2,1,0:T(8,128)}) conditional(s32[]{:T(128)} %convert_element_type.273, () %tuple.129, (s32[2,2048]{1,0:T(2,128)S(1)}, s32[]{:T(128)}, pred[1,128]{1,0:T(4,128)(4,1)S(1)}, s32[1,2048]{1,0:T(1,128)S(1)}, s32[1,128]{1,0:T(1,128)S(1)}, /*index=5*/s32[1,2048]{1,0:T(1,128)S(1)}, ...), branch_computations={%region_6.7_spmd, %region_7.13_spmd.clone} | conditional | flops 1098833152 | bytes 35224720 | solution.py:157
  2056.8 110.7 %while.40 = (s32[]{:T(128)}, f32[1,4,8,128]{3,2,1,0:T(8,128)S(1)}, f32[1,4,8,128]{3,2,1,0:T(8,128)}, f32[1,4,8,128,128]{4,3,2,1,0:T(8,128)}, s32[1,128]{1,0:T(1,...) while((s32[]{:T(128)}, f32[1,4,8,128]{3,2,1,0:T(8,128)S(1)}, ...), condition=%wide.region_11.12_spmd.clone, body=%wide.region_8.11_spmd.clone.sunk | while | flops 1098832896 | bytes 35205864 | solution.py:155
  2064.6 4.6 fusion.86
  2069.2 5.1 fusion.89
  2076.2 7.3 bitcast_add_fusion.5
  2091.3 4.6 fusion.86
  2095.9 5.1 fusion.89
  2103.6 7.9 bitcast_add_fusion.5
  2119.2 4.6 fusion.86
  2123.9 5.1 fusion.89
  2131.6 7.9 bitcast_add_fusion.5
  2147.2 4.6 fusion.86
  2151.9 5.1 fusion.89
  2159.6 7.9 bitcast_add_fusion.5
  (499 shorter events, 366.9 us)
Async XLA Ops:
  6.5 6.4 copy-start.1
  6.5 7.5 copy-start.2
  15.4 35.0 %copy-start.3 = (s32[2,32]{1,0:T(2,128)S(1)}, s32[2,32]{1,0:T(2,128)}, u32[]{:S(2)}) copy-start(s32[2,32]{1,0:T(2,128)} %param.25) | copy-start | bytes 772
  56.7 1.9 copy-start.4
  58.6 71.3 %all-gather.7.cloned.1.call-start = ((), (), s32[]{:S(2)}) async-start(), calls=%async_computation | async-start | bytes 2228224 | tf_op jit(solution)/shard_map/while/body/eval_jaxpr/all_gather | solution.py:105
  58.7 4.7 collective-permute-start
  69.4 107.1 %all-gather.9.cloned.1.call-start = ((), (), s32[]{:S(2)}) async-start(), calls=%async_computation.1 | async-start | bytes 2228224 | tf_op jit(solution)/shard_map/while/body/eval_jaxpr/all_gather | solution.py:106
  69.4 4.0 copy-start
  188.7 164.3 %all-gather.7.cloned.1.call-start = ((), (), s32[]{:S(2)}) async-start(), calls=%async_computation | async-start | bytes 2228224 | tf_op jit(solution)/shard_map/while/body/eval_jaxpr/all_gather | solution.py:105
  190.0 5.8 collective-permute-start
  201.7 197.6 %all-gather.9.cloned.1.call-start = ((), (), s32[]{:S(2)}) async-start(), calls=%async_computation.1 | async-start | bytes 2228224 | tf_op jit(solution)/shard_map/while/body/eval_jaxpr/all_gather | solution.py:106
  201.8 4.0 copy-start
  411.6 174.9 %all-gather.7.cloned.1.call-start = ((), (), s32[]{:S(2)}) async-start(), calls=%async_computation | async-start | bytes 2228224 | tf_op jit(solution)/shard_map/while/body/eval_jaxpr/all_gather | solution.py:105
  412.9 5.8 collective-permute-start
  424.6 208.3 %all-gather.9.cloned.1.call-start = ((), (), s32[]{:S(2)}) async-start(), calls=%async_computation.1 | async-start | bytes 2228224 | tf_op jit(solution)/shard_map/while/body/eval_jaxpr/all_gather | solution.py:106
  424.7 4.0 copy-start
  645.1 177.8 %all-gather.7.cloned.1.call-start = ((), (), s32[]{:S(2)}) async-start(), calls=%async_computation | async-start | bytes 2228224 | tf_op jit(solution)/shard_map/while/body/eval_jaxpr/all_gather | solution.py:105
  646.4 5.8 collective-permute-start
  658.2 211.2 %all-gather.9.cloned.1.call-start = ((), (), s32[]{:S(2)}) async-start(), calls=%async_computation.1 | async-start | bytes 2228224 | tf_op jit(solution)/shard_map/while/body/eval_jaxpr/all_gather | solution.py:106
  658.2 4.0 copy-start
  881.6 177.8 %all-gather.7.cloned.1.call-start = ((), (), s32[]{:S(2)}) async-start(), calls=%async_computation | async-start | bytes 2228224 | tf_op jit(solution)/shard_map/while/body/eval_jaxpr/all_gather | solution.py:105
  882.9 5.8 collective-permute-start
  894.7 211.1 %all-gather.9.cloned.1.call-start = ((), (), s32[]{:S(2)}) async-start(), calls=%async_computation.1 | async-start | bytes 2228224 | tf_op jit(solution)/shard_map/while/body/eval_jaxpr/all_gather | solution.py:106
  894.7 4.0 copy-start
  1118.0 179.3 %all-gather.7.cloned.1.call-start = ((), (), s32[]{:S(2)}) async-start(), calls=%async_computation | async-start | bytes 2228224 | tf_op jit(solution)/shard_map/while/body/eval_jaxpr/all_gather | solution.py:105
  1119.3 5.8 collective-permute-start
  1131.0 212.6 %all-gather.9.cloned.1.call-start = ((), (), s32[]{:S(2)}) async-start(), calls=%async_computation.1 | async-start | bytes 2228224 | tf_op jit(solution)/shard_map/while/body/eval_jaxpr/all_gather | solution.py:106
  1131.1 4.0 copy-start
  1355.9 179.3 %all-gather.7.cloned.1.call-start = ((), (), s32[]{:S(2)}) async-start(), calls=%async_computation | async-start | bytes 2228224 | tf_op jit(solution)/shard_map/while/body/eval_jaxpr/all_gather | solution.py:105
  1357.2 5.8 collective-permute-start
  1368.9 212.6 %all-gather.9.cloned.1.call-start = ((), (), s32[]{:S(2)}) async-start(), calls=%async_computation.1 | async-start | bytes 2228224 | tf_op jit(solution)/shard_map/while/body/eval_jaxpr/all_gather | solution.py:106
  1369.0 4.0 copy-start
  1593.7 179.0 %all-gather.7.cloned.1.call-start = ((), (), s32[]{:S(2)}) async-start(), calls=%async_computation | async-start | bytes 2228224 | tf_op jit(solution)/shard_map/while/body/eval_jaxpr/all_gather | solution.py:105
  1595.0 114.3 %collective-permute-start = (bf16[1,128,4096]{2,1,0:T(8,128)(2,1)S(1)}, bf16[1,128,4096]{2,1,0:T(8,128)(2,1)S(1)}, u32[]{:S(2)}, u32[]{:S(2)}) collective-permute-start(bf16[1,128,4096]{2,1,0:T(8,128)(2,1)S(1)} %broadcast_select_fusion.7), channel_id=1, source_target_pairs={{0,16},{16,32},{32,48},{48,64},{64,80},{80,96},{96,112},{1,17},{17... | collective-permute-start | bytes 3145736 | tf_op jit(solution)/shard_map/while/body/eval_jaxpr/ppermute | solution.py:17
  1715.3 103.8 %all-gather.9.cloned.1.call-start = ((), (), s32[]{:S(2)}) async-start(), calls=%async_computation.1 | async-start | bytes 2228224 | tf_op jit(solution)/shard_map/while/body/eval_jaxpr/all_gather | solution.py:106
  1715.4 4.0 copy-start
  1939.9 70.5 %all-gather.7.cloned.1.call-start = ((), (), s32[]{:S(2)}) async-start(), calls=%async_computation | async-start | bytes 2228224 | tf_op jit(solution)/shard_map/while/body/eval_jaxpr/all_gather | solution.py:105
  1941.2 5.8 collective-permute-start
  1952.9 103.8 %all-gather.9.cloned.1.call-start = ((), (), s32[]{:S(2)}) async-start(), calls=%async_computation.1 | async-start | bytes 2228224 | tf_op jit(solution)/shard_map/while/body/eval_jaxpr/all_gather | solution.py:106
  1953.0 4.0 copy-start
Sparse Core Ops, SparseCore 0:
  69.5 60.4 all-gather.6
  132.1 44.3 all-gather.8
  201.9 151.1 all-gather.6
  355.0 44.3 all-gather.8
  424.8 161.7 all-gather.6
  588.5 44.3 all-gather.8
  658.3 164.5 all-gather.6
  825.0 44.3 all-gather.8
  894.8 164.5 all-gather.6
  1061.4 44.3 all-gather.8
  1131.1 166.0 all-gather.6
  1299.3 44.3 all-gather.8
  1369.0 166.0 all-gather.6
  1537.1 44.3 all-gather.8
  1715.4 57.2 all-gather.6
  1774.8 44.3 all-gather.8
  1953.0 57.2 all-gather.6
  2012.4 44.3 all-gather.8
where the time goes:
time: 2190 us; the launch traced here: 2180 us
  waiting for transfers between devices  1610 us (74%)
  local copies, waits for them, and re-layouts  215 us (10%)
  other arithmetic  171 us (8%)
  matrix products  164 us (7%)
    all_gather x9, waiting for transfers between devices, run_layer(): key_piece = lax.all_gather(key_rows, 'seq', axis=1, tiled=True)  1050 us
    all_gather x9, waiting for transfers between devices, run_layer(): value_piece = lax.all_gather(value_rows, 'seq', axis=1, tiled=True)  418 us
    ppermute x9, waiting for transfers between devices, from_behind(): return lax.ppermute(value, axis, pairs)  134 us
    dot_general x8, matrix products, update(): jnp.einsum('gkhrs,gskd->gkhrd', weights.astype(jnp.bfloat16), value_blk.r...  61.6 us
  transfers between devices with their start and end apart: 27, of which 27 were waited for; matrix products, arithmetic and copies ran while one was open for 5% of the time, Pallas kernels for 0%

commit v1 on v0

--- a/solution.py
+++ b/solution.py
@@ -9,6 +9,11 @@
 HD = 128
 SPAN = 64
 rope_base = 500000.0
+
+
+def swapped_in(array, axis, dim):
+    sent = jnp.stack([array] * lax.axis_size(axis))
+    return jnp.concatenate(lax.all_to_all(sent, axis, 0, 0), axis=dim)
 
 
 def from_behind(value, axis, by):
@@ -102,7 +107,7 @@
         start_top = jnp.full((per_pass, HK, ratio, row_count), -jnp.inf, jnp.float32)
         start_sum = jnp.zeros((per_pass, HK, ratio, row_count), jnp.float32)
         start_acc = jnp.zeros((per_pass, HK, ratio, row_count, HD), jnp.float32)
-        key_piece = lax.all_gather(key_rows, "seq", axis=1, tiled=True)
+        key_piece = swapped_in(key_rows, "seq", 1)
         value_piece = lax.all_gather(value_rows, "seq", axis=1, tiled=True)
         piece_len = key_piece.shape[1]
         block_len = math.gcd(piece_len, 512)

time: 2190 us -> 1880 us (0.86)
  waiting for transfers between devices: 1610 us -> 1230 us
  starting transfers between devices: 12 us -> 58.2 us
  local copies, waits for them, and re-layouts: 215 us -> 237 us
    all_gather x9 -> x0, waiting for transfers between devices: 1050 us -> none  [run_layer(): key_piece = lax.all_gather(key_rows, 'seq', axis=1, tiled=True)]
    all_gather x9, waiting for transfers between devices: 418 us -> 954 us  [run_layer(): value_piece = lax.all_gather(value_rows, 'seq', axis=1, tiled=True)]
    all_to_all x0 -> x9, waiting for transfers between devices: none -> 129 us  [swapped_in(): return jnp.concatenate(lax.all_to_all(sent, axis, 0, 0), axis=dim)]
    all_to_all x0 -> x9, starting transfers between devices: none -> 46.5 us  [swapped_in(): return jnp.concatenate(lax.all_to_all(sent, axis, 0, 0), axis=dim)]
  transfers between devices with their start and end apart: 27 -> 27, of which waited for: 27 -> 27; matrix products, arithmetic and copies ran while one was open for 5% -> 7% of each run, Pallas kernels for 0% -> 0%
where the time goes in v1:
time: 1880 us; the launch traced here: 1870 us
  waiting for transfers between devices  1230 us (65%)
  local copies, waits for them, and re-layouts  237 us (13%)
  other arithmetic  165 us (9%)
  matrix products  163 us (9%)
  starting transfers between devices  58.2 us (3%)
    all_gather x9, waiting for transfers between devices, run_layer(): value_piece = lax.all_gather(value_rows, 'seq', axis=1, tiled=True)  954 us
    ppermute x9, waiting for transfers between devices, from_behind(): return lax.ppermute(value, axis, pairs)  151 us
    all_to_all x9, waiting for transfers between devices, swapped_in(): return jnp.concatenate(lax.all_to_all(sent, axis, 0, 0), axis=dim)  129 us
    dot_general x8, matrix products, update(): jnp.einsum('gkhrs,gskd->gkhrd', weights.astype(jnp.bfloat16), value_blk.r...  61.4 us
    all_to_all x9, starting transfers between devices, swapped_in(): return jnp.concatenate(lax.all_to_all(sent, axis, 0, 0), axis=dim)  46.5 us
    reduce_sum x8, other arithmetic, update(): denominator = denominator * rescale + jnp.sum(weights, axis=-1)  40.5 us
    convert_element_type x18, local copies, waits for them, and re-layouts, run_layer(): return (widened + attended.astype(jnp.float32)).astype(jnp.bfloat16)  38.7 us
  transfers between devices with their start and end apart: 27, of which 27 were waited for; matrix products, arithmetic and copies ran while one was open for 7% of the time, Pallas kernels for 0%

profile of v1, /device:TPU:25, one launch (start us, length us, event | category | flops | bytes accessed | tf_op | source)
XLA Modules:
  0.0 1874.1 jit_solution(15160680657312818172)
XLA Ops:
  6.5 6.4 copy.41
  15.4 34.9 %gather_fusion.6 = s32[4096]{0:T(1024)S(1)} fusion(s32[2,2048]{1,0:T(2,128)S(1)} %bitcast_subtract_fusion, s32[4096]{0:T(1024)S(1)} %bitcast.248), kind=kCustom, calls=%fused_computation.6 | custom fusion | bytes 65536 | tf_op jit(solution)/shard_map/jit(take_along_axis)/gather | solution.py:54
  50.5 5.5 gather_fusion.5
  58.6 1809.0 %while.41 = (s32[]{:T(128)}, bf16[1,128,4096]{2,1,0:T(8,128)(2,1)}, bf16[2,128,4096]{2,1,0:T(8,128)(2,1)}, s32[]{:T(128)}, pred[]{:T(512)}, /*index=5*/bf16[2,12...) while((s32[]{:T(128)}, bf16[1,128,4096]{2,1,0:T(8,128)(2,1)}, ...), condition=%wide.region_12.15_spmd.clone, body=%wide.region_4.14_spmd.clone.sunk | while | flops 2188912640 | bytes 120110880 | solution.py:192
  75.6 7.8 all-to-all-start
  90.4 15.0 all-to-all-done
  105.3 36.5 %all-gather.6.cloned.1.call-done = bf16[2048,512]{1,0:T(8,128)(2,1)} async-done(((bf16[128,512]{1,0:T(8,128)(2,1)}), bf16[2048,512]{1,0:T(8,128)(2,1)}) %all-gather.6.cloned.1.call-update) | async-done | bytes 2097168 | tf_op jit(solution)/shard_map/while/body/eval_jaxpr/all_gather | solution.py:111
  156.6 4.5 collective-permute-done
  173.3 4.8 all-to-all-start
  185.1 14.3 all-to-all-done
  199.4 124.3 %all-gather.6.cloned.1.call-done = bf16[2048,512]{1,0:T(8,128)(2,1)} async-done(((bf16[128,512]{1,0:T(8,128)(2,1)}), bf16[2048,512]{1,0:T(8,128)(2,1)}) %all-gather.6.cloned.1.call-update) | async-done | bytes 2097168 | tf_op jit(solution)/shard_map/while/body/eval_jaxpr/all_gather | solution.py:111
  355.2 4.8 all-to-all-start
  366.9 14.3 all-to-all-done
  381.3 149.6 %all-gather.6.cloned.1.call-done = bf16[2048,512]{1,0:T(8,128)(2,1)} async-done(((bf16[128,512]{1,0:T(8,128)(2,1)}), bf16[2048,512]{1,0:T(8,128)(2,1)}) %all-gather.6.cloned.1.call-update) | async-done | bytes 2097168 | tf_op jit(solution)/shard_map/while/body/eval_jaxpr/all_gather | solution.py:111
  545.7 4.5 collective-permute-done
  562.3 4.8 all-to-all-start
  574.1 14.3 all-to-all-done
  588.5 141.8 %all-gather.6.cloned.1.call-done = bf16[2048,512]{1,0:T(8,128)(2,1)} async-done(((bf16[128,512]{1,0:T(8,128)(2,1)}), bf16[2048,512]{1,0:T(8,128)(2,1)}) %all-gather.6.cloned.1.call-update) | async-done | bytes 2097168 | tf_op jit(solution)/shard_map/while/body/eval_jaxpr/all_gather | solution.py:111
  761.8 4.8 all-to-all-start
  773.5 14.3 all-to-all-done
  787.8 144.5 %all-gather.6.cloned.1.call-done = bf16[2048,512]{1,0:T(8,128)(2,1)} async-done(((bf16[128,512]{1,0:T(8,128)(2,1)}), bf16[2048,512]{1,0:T(8,128)(2,1)}) %all-gather.6.cloned.1.call-update) | async-done | bytes 2097168 | tf_op jit(solution)/shard_map/while/body/eval_jaxpr/all_gather | solution.py:111
  947.2 4.5 collective-permute-done
  963.9 4.8 all-to-all-start
  975.7 14.3 all-to-all-done
  990.0 143.6 %all-gather.6.cloned.1.call-done = bf16[2048,512]{1,0:T(8,128)(2,1)} async-done(((bf16[128,512]{1,0:T(8,128)(2,1)}), bf16[2048,512]{1,0:T(8,128)(2,1)}) %all-gather.6.cloned.1.call-update) | async-done | bytes 2097168 | tf_op jit(solution)/shard_map/while/body/eval_jaxpr/all_gather | solution.py:111
  1148.4 4.5 collective-permute-done
  1165.1 4.8 all-to-all-start
  1176.9 13.0 all-to-all-done
  1189.8 150.9 %all-gather.6.cloned.1.call-done = bf16[2048,512]{1,0:T(8,128)(2,1)} async-done(((bf16[128,512]{1,0:T(8,128)(2,1)}), bf16[2048,512]{1,0:T(8,128)(2,1)}) %all-gather.6.cloned.1.call-update) | async-done | bytes 2097168 | tf_op jit(solution)/shard_map/while/body/eval_jaxpr/all_gather | solution.py:111
  1355.6 116.2 %collective-permute-done = bf16[1,128,4096]{2,1,0:T(8,128)(2,1)S(1)} collective-permute-done((bf16[1,128,4096]{2,1,0:T(8,128)(2,1)S(1)}, bf16[1,128,4096]{2,1,0:T(8,128)(2,1)S(1)}, u32[]{:S(2)}, u32[]{:S(2)}) %collective-permute-start) | collective-permute-done | bytes 1048608 | tf_op jit(solution)/shard_map/while/body/eval_jaxpr/ppermute | solution.py:22
  1483.9 4.8 all-to-all-start
  1495.7 15.0 all-to-all-done
  1510.7 32.2 %all-gather.6.cloned.1.call-done = bf16[2048,512]{1,0:T(8,128)(2,1)} async-done(((bf16[128,512]{1,0:T(8,128)(2,1)}), bf16[2048,512]{1,0:T(8,128)(2,1)}) %all-gather.6.cloned.1.call-update) | async-done | bytes 2097168 | tf_op jit(solution)/shard_map/while/body/eval_jaxpr/all_gather | solution.py:111
  1542.8 113.8 %conditional.3 = (f32[1,4,8,128]{3,2,1,0:T(8,128)}, f32[1,4,8,128,128]{4,3,2,1,0:T(8,128)}) conditional(s32[]{:T(128)} %convert_element_type.271, () %tuple.131, (bf16[16,1,128,512]{2,3,1,0:T(8,128)(2,1)}, s32[2,2048]{1,0:T(2,128)S(1)}, s32[]{:T(128)}, pred[1,128]{1,0:T(4,128)(4,1)S(1)}, s32[1,2048]{1,0:T(1,128)S(1)}, ...), branch_computations={%region_6.7_spmd, %region_7.13_spmd.clone} | conditional | flops 1098833152 | bytes 39419024 | solution.py:162
  1546.1 110.6 %while.40 = (s32[]{:T(128)}, f32[1,4,8,128]{3,2,1,0:T(8,128)S(1)}, f32[1,4,8,128]{3,2,1,0:T(8,128)}, f32[1,4,8,128,128]{4,3,2,1,0:T(8,128)}, s32[1,128]{1,0:T(1,...) while((s32[]{:T(128)}, f32[1,4,8,128]{3,2,1,0:T(8,128)S(1)}, ...), condition=%wide.region_11.12_spmd.clone, body=%wide.region_8.11_spmd.clone.sunk | while | flops 1098832896 | bytes 35205864 | solution.py:160
  1553.9 4.6 fusion.87
  1558.5 5.1 fusion.90
  1565.5 7.2 bitcast_add_fusion.5
  1580.5 4.6 fusion.87
  1585.2 5.1 fusion.90
  1592.9 7.8 bitcast_add_fusion.5
  1608.5 4.6 fusion.87
  1613.2 5.1 fusion.90
  1620.9 7.8 bitcast_add_fusion.5
  1636.5 4.6 fusion.87
  1641.1 5.1 fusion.90
  1648.8 7.8 bitcast_add_fusion.5
  1686.0 4.8 all-to-all-start
  1697.8 15.0 all-to-all-done
  1712.7 31.0 %all-gather.6.cloned.1.call-done = bf16[2048,512]{1,0:T(8,128)(2,1)} async-done(((bf16[128,512]{1,0:T(8,128)(2,1)}), bf16[2048,512]{1,0:T(8,128)(2,1)}) %all-gather.6.cloned.1.call-update) | async-done | bytes 2097168 | tf_op jit(solution)/shard_map/while/body/eval_jaxpr/all_gather | solution.py:111
  1743.7 113.8 %conditional.3 = (f32[1,4,8,128]{3,2,1,0:T(8,128)}, f32[1,4,8,128,128]{4,3,2,1,0:T(8,128)}) conditional(s32[]{:T(128)} %convert_element_type.271, () %tuple.131, (bf16[16,1,128,512]{2,3,1,0:T(8,128)(2,1)}, s32[2,2048]{1,0:T(2,128)S(1)}, s32[]{:T(128)}, pred[1,128]{1,0:T(4,128)(4,1)S(1)}, s32[1,2048]{1,0:T(1,128)S(1)}, ...), branch_computations={%region_6.7_spmd, %region_7.13_spmd.clone} | conditional | flops 1098833152 | bytes 39419024 | solution.py:162
  1747.0 110.6 %while.40 = (s32[]{:T(128)}, f32[1,4,8,128]{3,2,1,0:T(8,128)S(1)}, f32[1,4,8,128]{3,2,1,0:T(8,128)}, f32[1,4,8,128,128]{4,3,2,1,0:T(8,128)}, s32[1,128]{1,0:T(1,...) while((s32[]{:T(128)}, f32[1,4,8,128]{3,2,1,0:T(8,128)S(1)}, ...), condition=%wide.region_11.12_spmd.clone, body=%wide.region_8.11_spmd.clone.sunk | while | flops 1098832896 | bytes 35205864 | solution.py:160
  1754.8 4.6 fusion.87
  1759.4 5.1 fusion.90
  1766.4 7.2 bitcast_add_fusion.5
  1781.4 4.6 fusion.87
  1786.1 5.1 fusion.90
  1793.8 7.8 bitcast_add_fusion.5
  1809.4 4.6 fusion.87
  1814.1 5.1 fusion.90
  1821.8 7.8 bitcast_add_fusion.5
  1837.4 4.6 fusion.87
  1842.0 5.1 fusion.90
  1849.7 7.8 bitcast_add_fusion.5
  (501 shorter events, 423.3 us)
Async XLA Ops:
  6.5 6.4 copy-start.1
  6.5 7.5 copy-start.2
  15.4 35.0 %copy-start.3 = (s32[2,32]{1,0:T(2,128)S(1)}, s32[2,32]{1,0:T(2,128)}, u32[]{:S(2)}) copy-start(s32[2,32]{1,0:T(2,128)} %param.25) | copy-start | bytes 772
  56.7 1.9 copy-start.4
  58.6 83.2 %all-gather.6.cloned.1.call-start = ((), (), s32[]{:S(2)}) async-start(), calls=%async_computation.1 | async-start | bytes 2228224 | tf_op jit(solution)/shard_map/while/body/eval_jaxpr/all_gather | solution.py:111
  58.7 4.7 collective-permute-start
  75.6 8.0 copy-start
  75.6 29.7 %all-to-all-start = ((bf16[16,1,128,512]{2,3,1,0:T(8,128)(2,1)}), bf16[16,1,128,512]{2,3,1,0:T(8,128)(2,1)}, u32[]{:S(2)}, u32[]{:S(2)}) async-start(bf16[16,1,128,512]{2,3,1,0:T(8,128)(2,1)} %stack.7), calls=%async_computation | async-start | bytes 4194304 | tf_op jit(solution)/shard_map/while/body/eval_jaxpr/all_to_all | solution.py:16
  154.0 169.6 %all-gather.6.cloned.1.call-start = ((), (), s32[]{:S(2)}) async-start(), calls=%async_computation.1 | async-start | bytes 2228224 | tf_op jit(solution)/shard_map/while/body/eval_jaxpr/all_gather | solution.py:111
  155.3 5.8 collective-permute-start
  173.3 5.1 copy-start
  173.3 26.1 %all-to-all-start = ((bf16[16,1,128,512]{2,3,1,0:T(8,128)(2,1)}), bf16[16,1,128,512]{2,3,1,0:T(8,128)(2,1)}, u32[]{:S(2)}, u32[]{:S(2)}) async-start(bf16[16,1,128,512]{2,3,1,0:T(8,128)(2,1)} %stack.7), calls=%async_computation | async-start | bytes 4194304 | tf_op jit(solution)/shard_map/while/body/eval_jaxpr/all_to_all | solution.py:16
  335.9 195.0 %all-gather.6.cloned.1.call-start = ((), (), s32[]{:S(2)}) async-start(), calls=%async_computation.1 | async-start | bytes 2228224 | tf_op jit(solution)/shard_map/while/body/eval_jaxpr/all_gather | solution.py:111
  337.2 5.8 collective-permute-start
  355.2 5.1 copy-start
  355.2 26.1 %all-to-all-start = ((bf16[16,1,128,512]{2,3,1,0:T(8,128)(2,1)}), bf16[16,1,128,512]{2,3,1,0:T(8,128)(2,1)}, u32[]{:S(2)}, u32[]{:S(2)}) async-start(bf16[16,1,128,512]{2,3,1,0:T(8,128)(2,1)} %stack.7), calls=%async_computation | async-start | bytes 4194304 | tf_op jit(solution)/shard_map/while/body/eval_jaxpr/all_to_all | solution.py:16
  543.1 187.2 %all-gather.6.cloned.1.call-start = ((), (), s32[]{:S(2)}) async-start(), calls=%async_computation.1 | async-start | bytes 2228224 | tf_op jit(solution)/shard_map/while/body/eval_jaxpr/all_gather | solution.py:111
  544.4 5.8 collective-permute-start
  562.3 5.1 copy-start
  562.3 26.1 %all-to-all-start = ((bf16[16,1,128,512]{2,3,1,0:T(8,128)(2,1)}), bf16[16,1,128,512]{2,3,1,0:T(8,128)(2,1)}, u32[]{:S(2)}, u32[]{:S(2)}) async-start(bf16[16,1,128,512]{2,3,1,0:T(8,128)(2,1)} %stack.7), calls=%async_computation | async-start | bytes 4194304 | tf_op jit(solution)/shard_map/while/body/eval_jaxpr/all_to_all | solution.py:16
  742.5 189.9 %all-gather.6.cloned.1.call-start = ((), (), s32[]{:S(2)}) async-start(), calls=%async_computation.1 | async-start | bytes 2228224 | tf_op jit(solution)/shard_map/while/body/eval_jaxpr/all_gather | solution.py:111
  743.8 5.8 collective-permute-start
  761.7 5.1 copy-start
  761.8 26.1 %all-to-all-start = ((bf16[16,1,128,512]{2,3,1,0:T(8,128)(2,1)}), bf16[16,1,128,512]{2,3,1,0:T(8,128)(2,1)}, u32[]{:S(2)}, u32[]{:S(2)}) async-start(bf16[16,1,128,512]{2,3,1,0:T(8,128)(2,1)} %stack.7), calls=%async_computation | async-start | bytes 4194304 | tf_op jit(solution)/shard_map/while/body/eval_jaxpr/all_to_all | solution.py:16
  944.6 189.0 %all-gather.6.cloned.1.call-start = ((), (), s32[]{:S(2)}) async-start(), calls=%async_computation.1 | async-start | bytes 2228224 | tf_op jit(solution)/shard_map/while/body/eval_jaxpr/all_gather | solution.py:111
  945.9 5.8 collective-permute-start
  963.9 5.1 copy-start
  963.9 26.1 %all-to-all-start = ((bf16[16,1,128,512]{2,3,1,0:T(8,128)(2,1)}), bf16[16,1,128,512]{2,3,1,0:T(8,128)(2,1)}, u32[]{:S(2)}, u32[]{:S(2)}) async-start(bf16[16,1,128,512]{2,3,1,0:T(8,128)(2,1)} %stack.7), calls=%async_computation | async-start | bytes 4194304 | tf_op jit(solution)/shard_map/while/body/eval_jaxpr/all_to_all | solution.py:16
  1145.8 195.0 %all-gather.6.cloned.1.call-start = ((), (), s32[]{:S(2)}) async-start(), calls=%async_computation.1 | async-start | bytes 2228224 | tf_op jit(solution)/shard_map/while/body/eval_jaxpr/all_gather | solution.py:111
  1147.1 5.8 collective-permute-start
  1165.1 5.1 copy-start
  1165.1 24.7 %all-to-all-start = ((bf16[16,1,128,512]{2,3,1,0:T(8,128)(2,1)}), bf16[16,1,128,512]{2,3,1,0:T(8,128)(2,1)}, u32[]{:S(2)}, u32[]{:S(2)}) async-start(bf16[16,1,128,512]{2,3,1,0:T(8,128)(2,1)} %stack.7), calls=%async_computation | async-start | bytes 4194304 | tf_op jit(solution)/shard_map/while/body/eval_jaxpr/all_to_all | solution.py:16
  1353.0 189.9 %all-gather.6.cloned.1.call-start = ((), (), s32[]{:S(2)}) async-start(), calls=%async_computation.1 | async-start | bytes 2228224 | tf_op jit(solution)/shard_map/while/body/eval_jaxpr/all_gather | solution.py:111
  1354.3 117.5 %collective-permute-start = (bf16[1,128,4096]{2,1,0:T(8,128)(2,1)S(1)}, bf16[1,128,4096]{2,1,0:T(8,128)(2,1)S(1)}, u32[]{:S(2)}, u32[]{:S(2)}) collective-permute-start(bf16[1,128,4096]{2,1,0:T(8,128)(2,1)S(1)} %broadcast_select_fusion.7), channel_id=1, source_target_pairs={{0,16},{16,32},{32,48},{48,64},{64,80},{80,96},{96,112},{1,17},{17... | collective-permute-start | bytes 3145736 | tf_op jit(solution)/shard_map/while/body/eval_jaxpr/ppermute | solution.py:22
  1483.9 5.1 copy-start
  1483.9 26.7 %all-to-all-start = ((bf16[16,1,128,512]{2,3,1,0:T(8,128)(2,1)}), bf16[16,1,128,512]{2,3,1,0:T(8,128)(2,1)}, u32[]{:S(2)}, u32[]{:S(2)}) async-start(bf16[16,1,128,512]{2,3,1,0:T(8,128)(2,1)} %stack.7), calls=%async_computation | async-start | bytes 4194304 | tf_op jit(solution)/shard_map/while/body/eval_jaxpr/all_to_all | solution.py:16
  1666.7 77.0 %all-gather.6.cloned.1.call-start = ((), (), s32[]{:S(2)}) async-start(), calls=%async_computation.1 | async-start | bytes 2228224 | tf_op jit(solution)/shard_map/while/body/eval_jaxpr/all_gather | solution.py:111
  1668.0 5.8 collective-permute-start
  1686.0 5.1 copy-start
  1686.0 26.7 %all-to-all-start = ((bf16[16,1,128,512]{2,3,1,0:T(8,128)(2,1)}), bf16[16,1,128,512]{2,3,1,0:T(8,128)(2,1)}, u32[]{:S(2)}, u32[]{:S(2)}) async-start(bf16[16,1,128,512]{2,3,1,0:T(8,128)(2,1)} %stack.7), calls=%async_computation | async-start | bytes 4194304 | tf_op jit(solution)/shard_map/while/body/eval_jaxpr/all_to_all | solution.py:16
Sparse Core Ops, SparseCore 0:
  68.9 72.8 all-gather.5
  166.6 157.0 all-gather.5
  348.5 182.3 all-gather.5
  555.6 174.5 all-gather.5
  755.0 177.3 all-gather.5
  957.2 176.3 all-gather.5
  1158.4 182.3 all-gather.5
  1477.2 65.5 all-gather.5
  1679.3 64.4 all-gather.5
